TPU v7x, 128 devices: a whole 4x4x4 slice. The times are simulated.
128 devices in a mesh: grp: 2 (over y_hi), row: 64 (over z, y_lo, x, core).
Axes of the slice: x: 4, y: 4 (y_hi: 2, y_lo: 2; y = y_hi * 2 + y_lo), z: 4, core: 2. Of those that a mesh axis runs over, the one named last changes fastest.
Arguments:
- features: bfloat16 [65536, 256], P(('grp', 'row')), may hold values from -6 to 6
- weight: bfloat16 [256, 256], replicated, may hold values from -0.375 to 0.375
- block_vals: bfloat16 [2, 512, 16, 128, 128], P('grp', 'row'), may hold values from -0.125 to 0.125
- block_cols: int32 [2, 512, 16], P('grp', 'row'), may hold values from 0 to 255, as said below
- block_count: int32 [2, 512], P('grp', 'row'), may hold values from 1 to 16, as said below
- cotangent: bfloat16 [65536, 256], P(('grp', 'row')), may hold values from -6 to 6
Outputs:
- activated: bfloat16 [65536, 256], P(('grp', 'row'))
- weight_grad: float32 [256, 256], replicated
- input_grad: bfloat16 [65536, 256], P(('grp', 'row'))
Inputs may be any that keep to these rules, and one draw needn't show every extreme that they name: `block_cols`: within one destination row block the 16 column blocks are distinct and ascending. `block_count`: in every draw some device holds 16 live slots in each of its row blocks.
All inputs are finite; a program needn't handle non-finite values.
Results may differ from a plain program's by a relative error of at most 0.0062.
Values may be sent and summed in bfloat16 or wider, within the bound.
No kernel may reach another device: no remote copies, remote signals or barrier semaphores. Data moves between devices by JAX's collectives and lax.ppermute only.
A program may use at most 128 MiB of HBM per device.

v0:
```python
import math
import jax
import jax.numpy as jnp
from jax import lax
from jax.sharding import PartitionSpec as P


def silu_slope(pre):
    sigma = jax.nn.sigmoid(pre)
    return sigma * (1.0 + pre * (1.0 - sigma))


def body(features, weight, block_vals, block_cols, block_count, cotangent):
    rows_dev, width = features.shape
    block = block_vals.shape[-1]
    slot_total = block_vals.shape[2]
    groups = lax.axis_size("grp")
    members = lax.axis_size("row")
    verts = rows_dev * groups * members
    slots = jnp.arange(slot_total)
    gathered = lax.all_gather(features, "row", axis=0, tiled=True)
    col_blocks = gathered.shape[0] // block
    panel_blocks = gathered.reshape(col_blocks, block, width)

    def aggregate(items):
        values, columns, count = items
        masked = jnp.where((slots < count)[:, None, None], values, jnp.zeros_like(values))
        picked = panel_blocks[columns]
        return jnp.einsum("kij,kjf->if", masked, picked, preferred_element_type=jnp.float32)

    partial_value = lax.map(aggregate, (block_vals[0], block_cols[0], block_count[0])).reshape(
        -1, width
    )
    summed = lax.psum_scatter(partial_value, "grp", scatter_dimension=0, tiled=True)
    aggregated = summed.astype(jnp.bfloat16)
    pre = jnp.dot(aggregated, weight, preferred_element_type=jnp.float32)
    activated = jax.nn.silu(pre).astype(jnp.bfloat16)
    pre_grad = (cotangent.astype(jnp.float32) * silu_slope(pre)).astype(jnp.bfloat16)
    local_grad = jnp.dot(aggregated.T, pre_grad, preferred_element_type=jnp.float32)
    own_grad = jnp.dot(pre_grad, weight.T, preferred_element_type=jnp.float32).astype(jnp.bfloat16)
    rows_grad = lax.all_gather(own_grad, "grp", axis=0, tiled=True)
    weight_grad = lax.psum(local_grad, ("grp", "row")) * (1.0 / math.sqrt(verts))
    by_block = rows_grad.reshape(-1, block, width)

    def spread(carry, items):
        values, columns, count, grad_block = items
        masked = jnp.where((slots < count)[:, None, None], values, jnp.zeros_like(values))
        contrib = jnp.einsum("kij,if->kjf", masked, grad_block, preferred_element_type=jnp.float32)
        return (carry.at[columns].add(contrib), None)

    total, unused = lax.scan(
        spread,
        jnp.zeros((col_blocks, block, width), jnp.float32),
        (block_vals[0], block_cols[0], block_count[0], by_block),
    )
    term = total.reshape(-1, width)
    input_grad = lax.psum_scatter(term, "row", scatter_dimension=0, tiled=True).astype(jnp.bfloat16)
    return (activated, weight_grad, input_grad)


def solution(mesh):
    placed = (
        P(("grp", "row"), None),
        P(),
        P("grp", "row", None, None, None),
        P("grp", "row", None),
        P("grp", "row"),
        P(("grp", "row"), None),
    )
    return jax.shard_map(
        body,
        mesh=mesh,
        in_specs=placed,
        out_specs=(P(("grp", "row"), None), P(), P(("grp", "row"), None)),
        check_vma=False,
    )
```

profile of v0, /device:TPU:0, one launch (start us, length us, event | category | flops | bytes accessed | tf_op | source)
XLA Modules:
  0.0 743.3 jit_solution(15940612499893916046)
XLA Ops:
  8.0 127.3 %all-gather.2.cloned.1.call-done = bf16[32768,256]{1,0:T(8,128)(2,1)} async-done(((bf16[512,256]{1,0:T(8,128)(2,1)}), bf16[32768,256]{1,0:T(8,128)(2,1)}) %all-gather.2.cloned.1.call-update) | async-done | bytes 16777232 | tf_op jit(solution)/shard_map/all_gather | solution.py:21
  135.3 88.4 %while.22 = (s32[]{:T(128)}, f32[8,128,256]{2,1,0:T(8,128)}, s32[8]{0:T(128)}, bf16[8,16,128,128]{3,2,1,0:T(8,128)(2,1)}, s32[8,16]{1,0:T(8,128)}, /*index=5*/bf16[256,128,256]{2,1,0:T(8,128)(2,1)}, s32[]{:T(128)}) while((s32[]{:T(128)}, f32[8,128,256]{2,1,0:T(8,128)}, s32[8]{0:T(128)}, bf16[8,16,128,128]{3,2,1,0:T(8,128)(2,1)}, ...), condition=%wide.region_1.2_spmd.clone, body=%wide.region_0.1_spmd.clone.sunk | while | flops 134480960 | bytes 3806601 | solution.py:31
  135.3 1.2 dynamic_slice.67
  137.9 6.4 gather_fusion
  144.3 2.1 fusion.42
  146.3 1.2 dynamic_slice.67
  148.9 6.4 gather_fusion
  155.3 2.1 fusion.42
  157.4 1.2 dynamic_slice.67
  160.0 6.4 gather_fusion
  166.4 2.1 fusion.42
  168.4 1.2 dynamic_slice.67
  171.0 6.4 gather_fusion
  177.4 2.1 fusion.42
  182.1 6.4 gather_fusion
  188.5 2.0 fusion.42
  193.1 6.4 gather_fusion
  199.5 2.1 fusion.42
  204.1 6.4 gather_fusion
  210.5 2.1 fusion.42
  215.2 6.4 gather_fusion
  221.6 2.1 fusion.42
  223.7 6.5 copy.9
  230.2 17.2 %reduce-scatter.3.cloned.1.call-done = f32[512,256]{1,0:T(8,128)} async-done(((f32[1024,256]{1,0:T(8,128)}), f32[512,256]{1,0:T(8,128)}) %reduce-scatter.3.cloned.1.call-update) | async-done | bytes 524304 | tf_op jit(solution)/shard_map/reduce_scatter | solution.py:34
  247.4 2.2 multiply_convert_fusion
  250.9 10.2 %all_gather.7 = bf16[1024,256]{1,0:T(8,128)(2,1)S(1)} all-gather(bf16[512,256]{1,0:T(8,128)(2,1)S(1)} %convolution_convert_fusion), channel_id=1, replica_groups=mesh['grp'=2,'row'=64] {'grp'}, dimensions={0}, use_global_device_ids=true | all-gather | bytes 786432 | tf_op jit(solution)/shard_map/all_gather | solution.py:41
  261.1 11.2 %broadcast_in_dim.28 = f32[256,128,256]{2,1,0:T(8,128)} broadcast(f32[]{:T(128)} %constant.27.clone.1), dimensions={} | broadcast | bytes 33554436 | tf_op jit(solution)/shard_map/broadcast_in_dim | solution.py:53
  272.4 63.8 %while.23 = (s32[]{:T(128)}, f32[256,128,256]{2,1,0:T(8,128)}, s32[8,16]{1,0:T(8,128)}, s32[8]{0:T(128)S(1)}, bf16[8,16,128,128]{2,3,1,0:T(8,128)(2,1)}, /*index=5*/bf16[8,128,256]{2,1,0:T(8,128)(2,1)S(1)}, s32[]{:T(128)}) while((s32[]{:T(128)}, f32[256,128,256]{2,1,0:T(8,128)}, s32[8,16]{1,0:T(8,128)}, s32[8]{0:T(128)S(1)}, ...), condition=%wide.region_6.7_spmd.clone, body=%wide.region_4.6_spmd.clone.sunk | while | flops 135004224 | bytes 8980281 | solution.py:51
  274.2 1.5 fusion.46
  275.7 4.6 scatter_fusion
  282.2 1.5 fusion.46
  283.7 4.6 scatter_fusion
  290.2 1.5 fusion.46
  291.7 4.6 scatter_fusion
  298.2 1.5 fusion.46
  299.7 4.6 scatter_fusion
  306.2 1.5 fusion.46
  307.7 4.6 scatter_fusion
  314.1 1.5 fusion.46
  315.7 4.6 scatter_fusion
  322.1 1.5 fusion.46
  323.6 4.6 scatter_fusion
  330.1 1.5 fusion.46
  331.6 4.6 scatter_fusion
  336.2 58.5 %all-reduce.2.cloned.1.call-done = f32[256,256]{1,0:T(8,128)} async-done(((f32[256,256]{1,0:T(8,128)}), f32[256,256]{1,0:T(8,128)}) %all-reduce.2.cloned.1.call-update) | async-done | bytes 262160 | tf_op jit(solution)/shard_map/psum | solution.py:42
  394.8 1.7 broadcast_multiply_fusion
  396.5 338.6 %reduce-scatter.5.cloned.1.call-done = f32[512,256]{1,0:T(8,128)} async-done(((f32[32768,256]{1,0:T(8,128)}), f32[512,256]{1,0:T(8,128)}) %reduce-scatter.5.cloned.1.call-update) | async-done | bytes 524304 | tf_op jit(solution)/shard_map/reduce_scatter | solution.py:57
  735.0 1.8 convert_element_type.23
  (71 shorter events, 32.6 us)
Async XLA Ops:
  7.2 240.2 %copy-start = (bf16[256,256]{1,0:T(8,128)(2,1)S(1)}, bf16[256,256]{1,0:T(8,128)(2,1)}, u32[]{:S(2)}) copy-start(bf16[256,256]{1,0:T(8,128)(2,1)} %param.11) | copy-start | bytes 393220
  7.2 128.1 %all-gather.2.cloned.1.call-start = ((), (), s32[]{:S(2)}) async-start(), calls=%async_computation.2 | async-start | bytes 17039360 | tf_op jit(solution)/shard_map/all_gather | solution.py:21
  7.9 239.5 %reduce-scatter.3.cloned.1.call-start = ((), (), s32[]{:S(2)}) async-start(), calls=%async_computation.3 | async-start | bytes 1572864 | tf_op jit(solution)/shard_map/reduce_scatter | solution.py:34
  223.7 23.7 %copy-start.2 = (bf16[512,256]{1,0:T(8,128)(2,1)S(1)}, bf16[512,256]{1,0:T(8,128)(2,1)}, u32[]{:S(2)}) copy-start(bf16[512,256]{1,0:T(8,128)(2,1)} %param.15) | copy-start | bytes 786436
  223.7 171.1 %all-reduce.2.cloned.1.call-start = ((), (), s32[]{:S(2)}) async-start(), calls=%async_computation.4 | async-start | bytes 524288 | tf_op jit(solution)/shard_map/psum | solution.py:42
  247.4 2.5 copy-start.1
  250.9 484.1 %reduce-scatter.5.cloned.1.call-start = ((), (), s32[]{:S(2)}) async-start(), calls=%async_computation.5 | async-start | bytes 34078720 | tf_op jit(solution)/shard_map/reduce_scatter | solution.py:57
  261.1 11.2 %copy-start.3 = (s32[8]{0:T(128)S(1)}, s32[8]{0:T(128)}, u32[]{:S(2)}) copy-start(s32[8]{0:T(128)} %get-tuple-element.273) | copy-start | bytes 100
Sparse Core Ops, SparseCore 0:
  9.7 125.4 all-gather.1
  223.8 23.5 reduce-scatter.2
  253.4 141.3 all-reduce.1
  397.2 337.8 reduce-scatter.4
where the time goes:
time: 746 us; the launch traced here: 743 us
  waiting for transfers between devices  542 us (73%)
  local copies, waits for them, and re-layouts  83.3 us (11%)
  other arithmetic  61.3 us (8%)
  matrix products  32 us (4%)
  between operations  13.8 us (2%)
  blocking collectives  10.2 us (1%)
    reduce_scatter x1, waiting for transfers between devices, body(): lax.psum_scatter(term, 'row', scatter_dimension=0, tiled=True)  339 us
    all_gather x1, waiting for transfers between devices, body(): gathered = lax.all_gather(features, 'row', axis=0, tiled=True)  127 us
    psum x1, waiting for transfers between devices, body(): lax.psum(local_grad, ('grp', 'row')) * (1.0 / math.sqrt(verts))  58.5 us
    gather x8, local copies, waits for them, and re-layouts, aggregate(): picked = panel_blocks[columns]  51.1 us
    scatter-add x8, other arithmetic, spread(): return (carry.at[columns].add(contrib), None)  36.9 us
    reduce_scatter x1, waiting for transfers between devices, body(): lax.psum_scatter(partial_value, 'grp', scatter_dimension=0, tiled=True)  17.2 us
    dot_general x8, matrix products, aggregate(): jnp.einsum('kij,kjf->if', masked, picked, preferred_element_type=jnp.floa...  16.4 us
  transfers between devices with their start and end apart: 4, of which 4 were waited for; matrix products, arithmetic and copies ran while one was open for 11% of the time, Pallas kernels for 0%

commit v1 on v0

--- a/solution.py
+++ b/solution.py
@@ -39,7 +39,7 @@
     local_grad = jnp.dot(aggregated.T, pre_grad, preferred_element_type=jnp.float32)
     own_grad = jnp.dot(pre_grad, weight.T, preferred_element_type=jnp.float32).astype(jnp.bfloat16)
     rows_grad = lax.all_gather(own_grad, "grp", axis=0, tiled=True)
-    weight_grad = lax.psum(local_grad, ("grp", "row")) * (1.0 / math.sqrt(verts))
+    weight_grad = lax.psum(lax.psum(local_grad, "row"), "grp") * (1.0 / math.sqrt(verts))
     by_block = rows_grad.reshape(-1, block, width)
 
     def spread(carry, items):

time: 746 us -> 1180 us (1.58)
  waiting for transfers between devices: 542 us -> 973 us
    psum x1 -> x2, waiting for transfers between devices: 58.5 us -> 491 us  [the longest x1 491 us: body(): lax.psum(local_grad, 'row')]
  transfers between devices with their start and end apart: 4 -> 5, of which waited for: 4 -> 4; matrix products, arithmetic and copies ran while one was open for 11% -> 7% of each run, Pallas kernels for 0% -> 0%
where the time goes in v1:
time: 1180 us
  waiting for transfers between devices  973 us (82%)
  local copies, waits for them, and re-layouts  83.3 us (7%)
  other arithmetic  62 us (5%)
  matrix products  33 us (3%)
  between operations  13.8 us (1%)
    psum x1, waiting for transfers between devices, body(): lax.psum(local_grad, 'row')  491 us
    reduce_scatter x1, waiting for transfers between devices, body(): lax.psum_scatter(term, 'row', scatter_dimension=0, tiled=True)  337 us
    all_gather x1, waiting for transfers between devices, body(): gathered = lax.all_gather(features, 'row', axis=0, tiled=True)  127 us
    gather x8, local copies, waits for them, and re-layouts, aggregate(): picked = panel_blocks[columns]  51.1 us
    scatter-add x8, other arithmetic, spread(): return (carry.at[columns].add(contrib), None)  36.9 us
  transfers between devices with their start and end apart: 5, of which 4 were waited for; matrix products, arithmetic and copies ran while one was open for 7% of the time, Pallas kernels for 0%

profile of v1, /device:TPU:0, one launch (start us, length us, event | category | flops | bytes accessed | tf_op | source)
XLA Modules:
  0.0 1175.7 jit_solution(8273087130929243374)
XLA Ops:
  8.0 127.3 %all-gather.2.cloned.1.call-done = bf16[32768,256]{1,0:T(8,128)(2,1)} async-done(((bf16[512,256]{1,0:T(8,128)(2,1)}), bf16[32768,256]{1,0:T(8,128)(2,1)}) %all-gather.2.cloned.1.call-update) | async-done | bytes 16777232 | tf_op jit(solution)/shard_map/all_gather | solution.py:21
  135.3 88.4 %while.22 = (s32[]{:T(128)}, f32[8,128,256]{2,1,0:T(8,128)}, s32[8]{0:T(128)}, bf16[8,16,128,128]{3,2,1,0:T(8,128)(2,1)}, s32[8,16]{1,0:T(8,128)}, /*index=5*/bf16[256,128,256]{2,1,0:T(8,128)(2,1)}, s32[]{:T(128)}) while((s32[]{:T(128)}, f32[8,128,256]{2,1,0:T(8,128)}, s32[8]{0:T(128)}, bf16[8,16,128,128]{3,2,1,0:T(8,128)(2,1)}, ...), condition=%wide.region_1.2_spmd.clone, body=%wide.region_0.1_spmd.clone.sunk | while | flops 134480960 | bytes 3806601 | solution.py:31
  135.3 1.2 dynamic_slice.67
  137.9 6.4 gather_fusion
  144.3 2.1 fusion.42
  146.3 1.2 dynamic_slice.67
  148.9 6.4 gather_fusion
  155.3 2.1 fusion.42
  157.4 1.2 dynamic_slice.67
  160.0 6.4 gather_fusion
  166.4 2.1 fusion.42
  171.0 6.4 gather_fusion
  177.4 2.1 fusion.42
  182.1 6.4 gather_fusion
  188.5 2.0 fusion.42
  193.1 6.4 gather_fusion
  199.5 2.1 fusion.42
  204.1 6.4 gather_fusion
  210.5 2.1 fusion.42
  215.2 6.4 gather_fusion
  221.6 2.0 fusion.42
  223.7 6.5 copy.9
  230.2 17.2 %reduce-scatter.3.cloned.1.call-done = f32[512,256]{1,0:T(8,128)} async-done(((f32[1024,256]{1,0:T(8,128)}), f32[512,256]{1,0:T(8,128)}) %reduce-scatter.3.cloned.1.call-update) | async-done | bytes 524304 | tf_op jit(solution)/shard_map/reduce_scatter | solution.py:34
  247.4 2.1 multiply_convert_fusion
  249.5 2.0 fusion.24
  251.9 10.2 all_gather.7
  262.1 491.0 %all-reduce.3.cloned.1.call-done = f32[256,256]{1,0:T(8,128)} async-done(((f32[256,256]{1,0:T(8,128)}), f32[256,256]{1,0:T(8,128)}) %all-reduce.3.cloned.1.call-update) | async-done | bytes 262160 | tf_op jit(solution)/shard_map/psum | solution.py:42
  753.2 11.2 broadcast_in_dim.28
  764.4 64.6 %while.23 = (s32[]{:T(128)}, f32[256,128,256]{2,1,0:T(8,128)}, s32[8,16]{1,0:T(8,128)}, s32[8]{0:T(128)S(1)}, bf16[8,16,128,128]{2,3,1,0:T(8,128)(2,1)}, /*index=5*/bf16[8,128,256]{2,1,0:T(8,128)(2,1)S(1)}, s32[]{:T(128)}) while((s32[]{:T(128)}, f32[256,128,256]{2,1,0:T(8,128)}, s32[8,16]{1,0:T(8,128)}, s32[8]{0:T(128)S(1)}, ...), condition=%wide.region_7.8_spmd.clone, body=%wide.region_5.7_spmd.clone.sunk | while | flops 135004224 | bytes 8980281 | solution.py:51
  766.3 1.5 fusion.46
  767.9 4.6 scatter_fusion
  774.4 1.5 fusion.46
  775.9 4.7 scatter_fusion
  782.5 1.5 fusion.46
  784.1 4.6 scatter_fusion
  790.6 1.5 fusion.46
  792.1 4.6 scatter_fusion
  798.7 1.5 fusion.46
  800.2 4.6 scatter_fusion
  806.7 1.5 fusion.46
  808.3 4.6 scatter_fusion
  814.8 1.5 fusion.46
  816.3 4.6 scatter_fusion
  822.9 1.5 fusion.46
  824.4 4.6 scatter_fusion
  829.0 1.7 broadcast_multiply_fusion
  830.7 336.6 %reduce-scatter.5.cloned.1.call-done = f32[512,256]{1,0:T(8,128)} async-done(((f32[32768,256]{1,0:T(8,128)}), f32[512,256]{1,0:T(8,128)}) %reduce-scatter.5.cloned.1.call-update) | async-done | bytes 524304 | tf_op jit(solution)/shard_map/reduce_scatter | solution.py:57
  1167.4 1.8 convert_element_type.23
  (74 shorter events, 33.7 us)
Async XLA Ops:
  7.2 240.2 %copy-start = (bf16[256,256]{1,0:T(8,128)(2,1)S(1)}, bf16[256,256]{1,0:T(8,128)(2,1)}, u32[]{:S(2)}) copy-start(bf16[256,256]{1,0:T(8,128)(2,1)} %param.11) | copy-start | bytes 393220
  7.2 128.1 %all-gather.2.cloned.1.call-start = ((), (), s32[]{:S(2)}) async-start(), calls=%async_computation.2 | async-start | bytes 17039360 | tf_op jit(solution)/shard_map/all_gather | solution.py:21
  7.9 239.5 %reduce-scatter.3.cloned.1.call-start = ((), (), s32[]{:S(2)}) async-start(), calls=%async_computation.3 | async-start | bytes 1572864 | tf_op jit(solution)/shard_map/reduce_scatter | solution.py:34
  223.7 23.7 %copy-start.2 = (bf16[512,256]{1,0:T(8,128)(2,1)S(1)}, bf16[512,256]{1,0:T(8,128)(2,1)}, u32[]{:S(2)}) copy-start(bf16[512,256]{1,0:T(8,128)(2,1)} %param.15) | copy-start | bytes 786436
  223.7 529.4 %all-reduce.3.cloned.1.call-start = ((), (), s32[]{:S(2)}) async-start(), calls=%async_computation.4 | async-start | bytes 524288 | tf_op jit(solution)/shard_map/psum | solution.py:42
  251.6 577.5 %all-reduce.5.cloned.1.call-start = ((), (), s32[]{:S(2)}) async-start(), calls=%async_computation.5 | async-start | bytes 524288 | tf_op jit(solution)/shard_map/psum | solution.py:42
  753.1 414.3 %reduce-scatter.5.cloned.1.call-start = ((), (), s32[]{:S(2)}) async-start(), calls=%async_computation.6 | async-start | bytes 34078720 | tf_op jit(solution)/shard_map/reduce_scatter | solution.py:57
  753.2 11.2 copy-start.3
  829.0 340.1 %copy-start.1 = (bf16[256,256]{1,0:T(8,128)(2,1)S(1)}, bf16[256,256]{1,0:T(8,128)(2,1)}, u32[]{:S(2)}) copy-start(bf16[256,256]{1,0:T(8,128)(2,1)} %param.11) | copy-start | bytes 393220
Sparse Core Ops, SparseCore 0:
  9.7 125.4 all-gather.1
  223.8 23.5 reduce-scatter.2
  251.7 501.3 all-reduce.2
  755.4 28.5 all-reduce.4
  829.1 338.1 reduce-scatter.4

commit v2 on v0

--- a/solution.py
+++ b/solution.py
@@ -39,7 +39,9 @@
     local_grad = jnp.dot(aggregated.T, pre_grad, preferred_element_type=jnp.float32)
     own_grad = jnp.dot(pre_grad, weight.T, preferred_element_type=jnp.float32).astype(jnp.bfloat16)
     rows_grad = lax.all_gather(own_grad, "grp", axis=0, tiled=True)
-    weight_grad = lax.psum(local_grad, ("grp", "row")) * (1.0 / math.sqrt(verts))
+    weight_grad = jnp.sum(lax.all_gather(local_grad, ("grp", "row")), axis=0) * (
+        1.0 / math.sqrt(verts)
+    )
     by_block = rows_grad.reshape(-1, block, width)
 
     def spread(carry, items):

time: 746 us -> 845 us (1.13)
  waiting for transfers between devices: 542 us -> 625 us
  other arithmetic: 61.3 us -> 73.5 us
    all_gather x0 -> x1, waiting for transfers between devices: none -> 144 us  [body(): lax.all_gather(local_grad, ('grp', 'row'))]
    psum x1 -> x0, waiting for transfers between devices: 58.5 us -> none  [body(): lax.psum(local_grad, ('grp', 'row')) * (1.0 / math.sqrt(verts))]
    reduce_sum x0 -> x1, other arithmetic: none -> 12.2 us  [body(): jnp.sum(lax.all_gather(local_grad, ('grp', 'row')), axis=0)]
    reduce_scatter x1, waiting for transfers between devices: 339 us -> 329 us  [body(): lax.psum_scatter(term, 'row', scatter_dimension=0, tiled=True)]
where the time goes in v2:
time: 845 us; the launch traced here: 843 us
  waiting for transfers between devices  625 us (74%)
  local copies, waits for them, and re-layouts  83.6 us (10%)
  other arithmetic  73.5 us (9%)
  matrix products  33 us (4%)
  blocking collectives  13.8 us (2%)
  between operations  13.8 us (2%)
    reduce_scatter x1, waiting for transfers between devices, body(): lax.psum_scatter(term, 'row', scatter_dimension=0, tiled=True)  329 us
    all_gather x1, waiting for transfers between devices, body(): lax.all_gather(local_grad, ('grp', 'row'))  144 us
    all_gather x1, waiting for transfers between devices, body(): gathered = lax.all_gather(features, 'row', axis=0, tiled=True)  127 us
    gather x8, local copies, waits for them, and re-layouts, aggregate(): picked = panel_blocks[columns]  51.1 us
    scatter-add x8, other arithmetic, spread(): return (carry.at[columns].add(contrib), None)  37.2 us
    reduce_scatter x1, waiting for transfers between devices, body(): lax.psum_scatter(partial_value, 'grp', scatter_dimension=0, tiled=True)  23.6 us
  transfers between devices with their start and end apart: 4, of which 4 were waited for; matrix products, arithmetic and copies ran while one was open for 11% of the time, Pallas kernels for 0%

profile of v2, /device:TPU:0, one launch (start us, length us, event | category | flops | bytes accessed | tf_op | source)
XLA Modules:
  0.0 842.7 jit_solution(5266381408285104476)
XLA Ops:
  8.0 127.3 %all-gather.4.cloned.1.call-done = bf16[32768,256]{1,0:T(8,128)(2,1)} async-done(((bf16[512,256]{1,0:T(8,128)(2,1)}), bf16[32768,256]{1,0:T(8,128)(2,1)}) %all-gather.4.cloned.1.call-update) | async-done | bytes 16777232 | tf_op jit(solution)/shard_map/all_gather | solution.py:21
  135.3 88.4 %while.22 = (s32[]{:T(128)}, f32[8,128,256]{2,1,0:T(8,128)}, s32[8]{0:T(128)}, bf16[8,16,128,128]{3,2,1,0:T(8,128)(2,1)}, s32[8,16]{1,0:T(8,128)}, /*index=5*/bf16[256,128,256]{2,1,0:T(8,128)(2,1)}, s32[]{:T(128)}) while((s32[]{:T(128)}, f32[8,128,256]{2,1,0:T(8,128)}, s32[8]{0:T(128)}, bf16[8,16,128,128]{3,2,1,0:T(8,128)(2,1)}, ...), condition=%wide.region_1.2_spmd.clone, body=%wide.region_0.1_spmd.clone.sunk | while | flops 134480960 | bytes 3806601 | solution.py:31
  135.3 1.3 dynamic_slice.67
  137.9 6.4 gather_fusion
  144.3 2.1 fusion.42
  146.4 1.2 dynamic_slice.67
  149.0 6.4 gather_fusion
  155.4 2.1 fusion.42
  157.4 1.2 dynamic_slice.67
  160.0 6.4 gather_fusion
  166.4 2.1 fusion.42
  171.1 6.4 gather_fusion
  177.5 2.1 fusion.42
  182.1 6.4 gather_fusion
  188.5 2.0 fusion.42
  193.1 6.4 gather_fusion
  199.5 2.1 fusion.42
  204.2 6.4 gather_fusion
  210.6 2.1 fusion.42
  215.2 6.4 gather_fusion
  221.6 2.1 fusion.42
  223.8 23.6 %reduce-scatter.3.cloned.1.call-done = f32[512,256]{1,0:T(8,128)} async-done(((f32[1024,256]{1,0:T(8,128)}), f32[512,256]{1,0:T(8,128)}) %reduce-scatter.3.cloned.1.call-update) | async-done | bytes 524304 | tf_op jit(solution)/shard_map/reduce_scatter | solution.py:34
  247.4 2.1 multiply_convert_fusion
  249.6 2.0 fusion.24
  251.6 6.5 copy.9
  258.4 13.8 %all_gather.15 = bf16[1024,256]{1,0:T(8,128)(2,1)S(1)} all-gather(bf16[512,256]{1,0:T(8,128)(2,1)S(1)} %convolution_convert_fusion), channel_id=1, replica_groups=mesh['grp'=2,'row'=64] {'grp'}, dimensions={0}, use_global_device_ids=true | all-gather | bytes 786432 | tf_op jit(solution)/shard_map/all_gather | solution.py:41
  272.2 11.3 %broadcast_in_dim.28 = f32[256,128,256]{2,1,0:T(8,128)} broadcast(f32[]{:T(128)} %constant.27.clone.1), dimensions={} | broadcast | bytes 33554436 | tf_op jit(solution)/shard_map/broadcast_in_dim | solution.py:55
  283.5 65.0 %while.23 = (s32[]{:T(128)}, f32[256,128,256]{2,1,0:T(8,128)}, s32[8,16]{1,0:T(8,128)}, s32[8]{0:T(128)S(1)}, bf16[8,16,128,128]{2,3,1,0:T(8,128)(2,1)}, /*index=5*/bf16[8,128,256]{2,1,0:T(8,128)(2,1)S(1)}, s32[]{:T(128)}) while((s32[]{:T(128)}, f32[256,128,256]{2,1,0:T(8,128)}, s32[8,16]{1,0:T(8,128)}, s32[8]{0:T(128)S(1)}, ...), condition=%wide.region_6.7_spmd.clone, body=%wide.region_4.6_spmd.clone.sunk | while | flops 135004224 | bytes 8980281 | solution.py:53
  285.4 1.5 fusion.46
  287.0 4.6 scatter_fusion
  293.5 1.5 fusion.46
  295.1 4.6 scatter_fusion
  301.6 1.5 fusion.46
  303.1 4.6 scatter_fusion
  309.7 1.5 fusion.46
  311.2 4.7 scatter_fusion
  317.9 1.5 fusion.46
  319.4 4.7 scatter_fusion
  326.1 1.5 fusion.46
  327.6 4.6 scatter_fusion
  334.2 1.5 fusion.46
  335.7 4.6 scatter_fusion
  342.3 1.5 fusion.46
  343.8 4.7 scatter_fusion
  348.5 144.3 %all-gather.6.cloned.1.call-done = f32[32768,256]{1,0:T(8,128)} async-done(((f32[256,256]{1,0:T(8,128)}), f32[32768,256]{1,0:T(8,128)}) %all-gather.6.cloned.1.call-update) | async-done | bytes 33554448 | tf_op jit(solution)/shard_map/all_gather | solution.py:42
  492.9 12.2 %reduce_sum.9 = f32[256,256]{1,0:T(8,128)S(1)} reduce(f32[128,256,256]{2,1,0:T(8,128)} %bitcast.70, f32[]{:T(128)} %constant.27.clone.1), dimensions={0}, to_apply=%region_3.4 | reduce | flops 8323072 | bytes 33816580 | tf_op jit(solution)/shard_map/reduce_sum | solution.py:42
  505.8 328.6 %reduce-scatter.5.cloned.1.call-done = f32[512,256]{1,0:T(8,128)} async-done(((f32[32768,256]{1,0:T(8,128)}), f32[512,256]{1,0:T(8,128)}) %reduce-scatter.5.cloned.1.call-update) | async-done | bytes 524304 | tf_op jit(solution)/shard_map/reduce_scatter | solution.py:59
  834.4 1.8 convert_element_type.23
  (72 shorter events, 34.5 us)
Async XLA Ops:
  7.2 240.2 %copy-start = (bf16[256,256]{1,0:T(8,128)(2,1)S(1)}, bf16[256,256]{1,0:T(8,128)(2,1)}, u32[]{:S(2)}) copy-start(bf16[256,256]{1,0:T(8,128)(2,1)} %param.11) | copy-start | bytes 393220
  7.2 128.1 %all-gather.4.cloned.1.call-start = ((), (), s32[]{:S(2)}) async-start(), calls=%async_computation.2 | async-start | bytes 17039360 | tf_op jit(solution)/shard_map/all_gather | solution.py:21
  7.9 239.5 %reduce-scatter.3.cloned.1.call-start = ((), (), s32[]{:S(2)}) async-start(), calls=%async_computation.3 | async-start | bytes 1572864 | tf_op jit(solution)/shard_map/reduce_scatter | solution.py:34
  135.3 112.1 %copy-start.2 = (bf16[512,256]{1,0:T(8,128)(2,1)S(1)}, bf16[512,256]{1,0:T(8,128)(2,1)}, u32[]{:S(2)}) copy-start(bf16[512,256]{1,0:T(8,128)(2,1)} %param.15) | copy-start | bytes 786436
  223.7 269.1 %all-gather.6.cloned.1.call-start = ((), (), s32[]{:S(2)}) async-start(), calls=%async_computation.5 | async-start | bytes 33816576 | tf_op jit(solution)/shard_map/all_gather | solution.py:42
  251.6 582.8 %reduce-scatter.5.cloned.1.call-start = ((), (), s32[]{:S(2)}) async-start(), calls=%async_computation.4 | async-start | bytes 34078720 | tf_op jit(solution)/shard_map/reduce_scatter | solution.py:59
  272.2 11.3 %copy-start.3 = (s32[8]{0:T(128)S(1)}, s32[8]{0:T(128)}, u32[]{:S(2)}) copy-start(s32[8]{0:T(128)} %get-tuple-element.273) | copy-start | bytes 100
  492.9 343.3 %copy-start.1 = (bf16[256,256]{1,0:T(8,128)(2,1)S(1)}, bf16[256,256]{1,0:T(8,128)(2,1)}, u32[]{:S(2)}) copy-start(bf16[256,256]{1,0:T(8,128)(2,1)} %param.11) | copy-start | bytes 393220
Sparse Core Ops, SparseCore 0:
  9.7 125.4 all-gather.3
  223.8 23.5 reduce-scatter.2
  251.7 241.0 all-gather.5
  495.2 339.1 reduce-scatter.4
